TPU v7x, 32 devices: a whole 2x2x4 slice. The times are simulated.
32 devices in a mesh: led: 4 (over y, x), row: 8 (over z, core).
Axes of the slice: x: 2, y: 2, z: 4, core: 2. Of those that a mesh axis runs over, the one named last changes fastest.
Arguments:
- spectrum: float32 [2, 4096, 4096], P(None, 'led', 'row'), may hold values from -6 to 6
- amplitudes: float32 [4, 2048, 2048], P('led', 'row'), may hold values from 0.2 to 3
- offsets: int32 [4, 2], replicated, may hold values from 0 to 2048
- coeffs: float32 [6], replicated, may hold values from -2.5 to 2.5
Outputs:
- updated: float32 [2, 4096, 4096], P(None, 'led', 'row')
All inputs are finite; a program needn't handle non-finite values.
Results may differ from a plain program's by a relative error of at most 0.0001.
Values sent between devices are 32-bit elements; how exact they have to be, the bound alone decides.
No kernel may reach another device: no remote copies, remote signals or barrier semaphores. Data moves between devices by JAX's collectives and lax.ppermute only.
A program may use at most 128 MiB of HBM per device.

v0:
```python
import math
import jax
import jax.numpy as jnp
from jax import lax
from jax.sharding import PartitionSpec as P

SOFTENING = 0.1
HIGHEST_PRECISION = lax.Precision.HIGHEST


def pupil_at(down_index, across_index, coeffs, centre):
    offset_down = down_index - centre
    offset_across = across_index - centre
    inside = offset_down * offset_down + offset_across * offset_across < centre * centre
    upper_norm = offset_down.astype(jnp.float32) * (1.0 / centre)
    lateral = offset_across.astype(jnp.float32) * (1.0 / centre)
    radial = upper_norm * upper_norm + lateral * lateral
    phases = (
        coeffs[0] * (2.0 * radial - 1.0)
        + coeffs[1] * (upper_norm * upper_norm - lateral * lateral)
        + coeffs[2] * (2.0 * upper_norm * lateral)
        + (3.0 * radial - 2.0) * (coeffs[3] * upper_norm + coeffs[4] * lateral)
        + coeffs[5] * (6.0 * radial * radial - 6.0 * radial + 1.0)
    )
    weight = jnp.where(inside, 1.0, 0.0).astype(jnp.float32)
    return (weight * jnp.cos(phases), weight * jnp.sin(phases))


def tables(outer_size, inner_size, direction):
    length = outer_size * inner_size
    angle_step = direction * 2.0 * math.pi / length
    first_index = jnp.arange(outer_size, dtype=jnp.int32)
    grid_first = first_index[:, None] * first_index[None, :] * inner_size % length
    angles_first = grid_first.astype(jnp.float32) * angle_step
    index_k = jnp.arange(outer_size, dtype=jnp.int32)[:, None, None]
    index_r = jnp.arange(inner_size, dtype=jnp.int32)[None, :, None]
    index_j = jnp.arange(inner_size, dtype=jnp.int32)[None, None, :]
    grid_second = index_r * (index_k + outer_size * index_j) % length
    angles_second = grid_second.astype(jnp.float32) * angle_step
    return (
        jnp.cos(angles_first),
        jnp.sin(angles_first),
        jnp.cos(angles_second),
        jnp.sin(angles_second),
    )


def transform(paired, inputs, middle, output, outer_size, inner_size, direction):
    first_re, first_im, second_re, second_im = tables(outer_size, inner_size, direction)
    scaling = 1.0 / math.sqrt(outer_size * inner_size)
    first_table = jnp.stack([jnp.stack([first_re, first_im]), jnp.stack([-first_im, first_re])])
    second_table = (
        jnp.stack([jnp.stack([second_re, second_im]), jnp.stack([-second_im, second_re])]) * scaling
    )
    middle_pair = jnp.einsum(
        "p" + inputs + ",pqtk->q" + middle, paired, first_table, precision=HIGHEST_PRECISION
    )
    return jnp.einsum(
        "p" + middle + ",pqkrj->q" + output, middle_pair, second_table, precision=HIGHEST_PRECISION
    )


def correct(field_re, field_im, measured):
    magnitude = jnp.sqrt(field_re * field_re + field_im * field_im + SOFTENING)
    factor = measured / magnitude
    return (field_re * factor - field_re, field_im * factor - field_im)


def on_device(spectrum, amplitudes, offsets, coeffs):
    led_count = lax.axis_size("led")
    row_count = lax.axis_size("row")
    led_index = lax.axis_index("led")
    row_index = lax.axis_index("row")
    size_rows = spectrum.shape[1]
    size_cols = spectrum.shape[2]
    window = amplitudes.shape[2]
    centre = window // 2
    block_rows = window // row_count
    outer_rows = window // led_count
    outer_cols = window // row_count
    row_shift = offsets[led_index, 0]
    col_shift = offsets[led_index, 1]
    measured = amplitudes[0]
    shape_cols = (2, block_rows, outer_cols, row_count)
    region = lax.all_gather(spectrum, "led", axis=1, tiled=True)
    band_rows = lax.dynamic_slice_in_dim(region, row_shift, window, 1)
    row_ids = jnp.arange(window, dtype=jnp.int32)[:, None]
    col_ids = (row_index * size_cols + jnp.arange(size_cols, dtype=jnp.int32))[None, :] - col_shift
    pupil_re, pupil_im = pupil_at(row_ids, col_ids, coeffs, centre)
    lit_re = pupil_re * band_rows[0] - pupil_im * band_rows[1]
    lit_im = pupil_re * band_rows[1] + pupil_im * band_rows[0]
    shape_rows = (2, outer_rows, led_count, size_cols)
    half = transform(
        jnp.stack([lit_re, lit_im]).reshape(shape_rows),
        "trc",
        "krc",
        "jkc",
        outer_rows,
        led_count,
        1.0,
    )
    stacked = half.reshape(2, window, size_cols)
    spread = lax.all_to_all(stacked, "row", split_axis=1, concat_axis=2, tiled=True)
    window_part = lax.dynamic_slice_in_dim(spread, col_shift, window, 2)
    field = transform(
        window_part.reshape(shape_cols), "ytr", "ykr", "yjk", outer_cols, row_count, 1.0
    )
    field = field.reshape(2, block_rows, window)
    diff_re, diff_im = correct(field[0], field[1], measured)
    back = transform(
        jnp.stack([diff_re, diff_im]).reshape(shape_cols),
        "ytr",
        "ykr",
        "yjk",
        outer_cols,
        row_count,
        -1.0,
    )
    padded = jnp.zeros((2, block_rows, row_count * size_cols), jnp.float32)
    padded = lax.dynamic_update_slice_in_dim(
        padded, back.reshape(2, block_rows, window), col_shift, 2
    )
    gathered_cols = lax.all_to_all(padded, "row", split_axis=2, concat_axis=1, tiled=True)
    spec = transform(
        gathered_cols.reshape(shape_rows), "trc", "krc", "jkc", outer_rows, led_count, -1.0
    ).reshape(2, window, size_cols)
    upd_re = pupil_re * spec[0] + pupil_im * spec[1]
    upd_im = pupil_re * spec[1] - pupil_im * spec[0]
    embedded = jnp.zeros((2, size_rows * led_count, size_cols), jnp.float32)
    embedded = lax.dynamic_update_slice_in_dim(embedded, jnp.stack([upd_re, upd_im]), row_shift, 1)
    summed = lax.psum_scatter(embedded, "led", scatter_dimension=1, tiled=True)
    return spectrum + summed


def solution(mesh):
    return jax.shard_map(
        on_device,
        mesh=mesh,
        in_specs=(P(None, "led", "row"), P("led", "row", None), P(), P()),
        out_specs=P(None, "led", "row"),
        check_vma=False,
    )
```

profile of v0, /device:TPU:0, one launch (start us, length us, event | category | flops | bytes accessed | tf_op | source)
XLA Modules:
  0.0 1087.1 jit_solution(2746678404710610124)
XLA Ops:
  6.5 0.7 all-gather.2.cloned.1.call-update
  7.3 0.7 constant_dynamic-slice_fusion
  11.7 3.3 copy.145
  15.7 0.7 fusion.86
  16.4 0.7 fusion.87
  17.1 0.7 convert_multiply_fusion.2
  17.9 3.9 fusion.69
  21.7 4.1 multiply_sine_fusion
  25.9 2.0 maximum_bitcast_fusion.15
  27.8 141.4 %all-gather.2.cloned.1.call-done = f32[2,4096,512]{2,1,0:T(8,128)} async-done(((f32[2,1024,512]{2,1,0:T(8,128)}), f32[2,4096,512]{2,1,0:T(8,128)}) %all-gather.2.cloned.1.call-update) | async-done | bytes 16777232 | tf_op jit(solution)/shard_map/all_gather | solution.py:85
  169.3 26.9 %multiply_subtract_fusion = (f32[1,2048,512]{2,1,0:T(8,128)}, f32[1,2048,512]{2,1,0:T(8,128)}) fusion(f32[2,4096,512]{2,1,0:T(8,128)} %all-gather.2.cloned.1.call-done, s32[]{:T(128)S(6)} %select_n.238, s32[]{:T(128)S(6)} %add.718, f32[]{:T(128)} %bitcast.6, f32[512]{0:T(512)S(1)} %get-tuple-element.53, f32[2048]{0:T(1024)S(1)} %get-tuple-element.58, ...), kind=kLoop, calls=%fused_computation.55 | loop fusion | flops 33554432 | bytes 16818200 | tf_op jit(solution)/shard_map/sub | solution.py:90
  196.1 7.9 stack.215
  204.1 5.5 copy.143
  209.6 7.7 stack.216
  217.3 3.7 copy.144
  221.4 28.3 %fusion.46 = f32[2,512,4,512,1]{3,1,2,0,4:T(8,128)} fusion(f32[1,512,4,512]{3,1,0,2:T(8,128)S(1)} %copy.144, f32[1,512,4,512]{3,1,0,2:T(8,128)S(1)} %copy-done.3, f32[1,2,512,512]{2,3,0,1:T(8,128)S(1)} %copy-done.4, f32[1,2,512,512]{2,3,0,1:T(8,128)S(1)} %get-tuple-element.17), kind=kOutput, calls=%fused_computation.58 | convolution fusion | flops 25772949504 | bytes 20971520 | tf_op jit(solution)/shard_map/ptrc,pqtk->qkrc/dot_general | solution.py:55
  249.7 32.7 %fusion.11 = f32[2,4,512,512]{3,1,0,2:T(4,128)S(1)} fusion(f32[2,2,512,4,4]{3,4,0,1,2:T(4,128)} %copy.145, f32[2,512,4,512,1]{3,1,2,0,4:T(8,128)} %fusion.46), kind=kOutput, calls=%fused_computation.19 | convolution fusion | flops 201326592 | bytes 16908288 | tf_op jit(solution)/shard_map/pkrc,pqkrj->qjkc/dot_general | solution.py:58
  282.4 4.9 copy.147
  287.2 16.5 %copy.148 = f32[2,2048,512]{2,0,1:T(2,128)} copy(f32[2,2048,512]{2,1,0:T(8,128)S(1)} %bitcast.186) | data formatting | bytes 16777216 | tf_op jit(solution)/shard_map/reshape | solution.py:102
  303.7 5.1 all-to-all-start
  310.9 4.4 copy.152
  315.3 1.9 copy.156
  317.2 4.4 copy.160
  322.3 1.0 fusion.73
  323.3 1.0 fusion.72
  324.3 1.0 multiply_sine_fusion.2
  325.4 1.0 multiply_sine_fusion.3
  326.4 1.1 maximum_bitcast_fusion.22
  327.6 165.1 %all-to-all-done = f32[2,2048,512]{2,0,1:T(2,128)} async-done(((f32[2,2048,512]{2,0,1:T(2,128)}), f32[2,2048,512]{2,0,1:T(2,128)}, u32[]{:S(2)}, u32[]{:S(2)}) %all-to-all-start) | async-done | bytes 8388640 | tf_op jit(solution)/shard_map/all_to_all | solution.py:103
  492.7 8.2 copy.149
  501.0 8.8 copy.150
  509.7 4.5 dynamic-slice_bitcast_fusion
  514.3 5.3 copy.151
  519.5 9.7 fusion.54
  529.3 7.0 fusion.47
  536.7 0.7 copy.154
  537.3 0.7 copy.155
  538.0 2.7 fusion.57
  540.8 3.1 copy.157
  543.8 1.8 copy.158
  545.6 9.1 fusion.53
  554.8 7.0 fusion.50
  561.8 2.4 copy.162
  564.2 5.4 broadcast_in_dim.15
  569.6 12.4 %copy_dynamic-update-slice_fusion = f32[2,256,4096]{1,0,2:T(2,128)} fusion(f32[2,256,4096]{1,0,2:T(2,128)} %broadcast_in_dim.15, s32[]{:T(128)S(6)} %select_n.239, f32[2,256,2048]{1,2,0:T(8,128)S(1)} %bitcast.190), kind=kLoop, calls=%fused_computation.52 | loop fusion | bytes 8388612 | tf_op jit(solution)/shard_map/dynamic_update_slice | solution.py:120
  582.1 5.0 all-to-all-start.1
  587.1 3.3 copy.168
  590.4 3.9 fusion.68
  594.3 4.1 multiply_sine_fusion.1
  598.4 1.9 maximum_bitcast_fusion.13
  600.4 170.5 %all-to-all-done.1 = f32[2,256,4096]{1,0,2:T(2,128)} async-done(((f32[2,256,4096]{1,0,2:T(2,128)}), f32[2,256,4096]{1,0,2:T(2,128)}, u32[]{:S(2)}, u32[]{:S(2)}) %all-to-all-start.1) | async-done | bytes 8388640 | tf_op jit(solution)/shard_map/all_to_all | solution.py:123
  770.9 7.3 copy.164
  778.2 13.3 %copy.165 = f32[2,8,256,512]{3,0,2,1:T(2,128)} copy(f32[2,8,256,512]{2,3,1,0:T(8,128)} %bitcast.188) | data formatting | bytes 16777216 | tf_op jit(solution)/shard_map/all_to_all | solution.py:123
  791.5 31.6 %fusion.41 = f32[2,512,4,512,1]{3,1,2,0,4:T(8,128)} fusion(f32[2,512,4,512]{3,0,2,1:T(2,128)} %bitcast.191, f32[1,2,512,512]{2,3,1,0:T(8,128)} %get-tuple-element.16, f32[1,2,512,512]{2,3,1,0:T(8,128)S(1)} %get-tuple-element.15), kind=kOutput, calls=%fused_computation.57 | convolution fusion | flops 25770852352 | bytes 20971520 | tf_op jit(solution)/shard_map/ptrc,pqtk->qkrc/dot_general | solution.py:55
  823.2 32.4 %fusion.14 = f32[2,4,512,512]{3,1,0,2:T(4,128)S(1)} fusion(f32[2,2,512,4,4]{3,4,0,1,2:T(4,128)} %copy.168, f32[2,512,4,512,1]{3,1,2,0,4:T(8,128)} %fusion.41), kind=kOutput, calls=%fused_computation.20 | convolution fusion | flops 201326592 | bytes 16908288 | tf_op jit(solution)/shard_map/pkrc,pqkrj->qjkc/dot_general | solution.py:58
  855.6 3.5 fusion.91
  859.0 3.5 copy.170
  862.6 1.4 copy.171
  863.9 23.1 %fusion.32 = (f32[1,2048,512]{2,1,0:T(8,128)S(1)}, f32[1,2048,512]{2,1,0:T(8,128)S(1)}) fusion(f32[1,4,512,512]{3,2,1,0:T(8,128)S(1)} %copy.171, f32[1,4,512,512]{3,2,1,0:T(8,128)S(1)} %copy.170, f32[]{:T(128)} %bitcast.6, f32[512]{0:T(512)S(1)} %get-tuple-element.53, f32[2048]{0:T(1024)S(1)} %get-tuple-element.58, f32[512]{0:T(512)S(1)} %get-tuple-element.54, ...), kind=kLoop, calls=%fused_computation.41 | loop fusion | flops 33554432 | bytes 16818192 | tf_op jit(solution)/shard_map/add | solution.py:127
  887.0 4.2 pad_maximum_fusion
  891.3 7.9 broadcast_in_dim.12
  899.2 22.7 %dynamic_update_slice.7 = f32[2,4096,512]{2,1,0:T(8,128)} dynamic-update-slice(f32[2,4096,512]{2,1,0:T(8,128)} %broadcast_in_dim.12, f32[2,2048,512]{2,1,0:T(8,128)} %pad_maximum_fusion, s32[]{:T(128)} %constant.100.clone.1, s32[]{:T(128)S(6)} %select_n.238, s32[]{:T(128)} %constant.100.clone.1) | dynamic-update-slice | bytes 16777220 | tf_op jit(solution)/shard_map/dynamic_update_slice | solution.py:130
  921.8 151.7 %reduce-scatter.2.cloned.1.call-done = f32[2,1024,512]{2,1,0:T(8,128)} async-done(((f32[2,4096,512]{2,1,0:T(8,128)}), f32[2,1024,512]{2,1,0:T(8,128)}) %reduce-scatter.2.cloned.1.call-update) | async-done | bytes 4194320 | tf_op jit(solution)/shard_map/reduce_scatter | solution.py:131
  1073.5 6.5 add.717
  (35 shorter events, 2.8 us)
Async XLA Ops:
  6.5 0.7 copy-start.6
  6.5 2.8 copy-start.5
  6.5 162.7 %all-gather.2.cloned.1.call-start = ((), (), s32[]{:S(2)}) async-start(), calls=%async_computation.3 | async-start | bytes 20971520 | tf_op jit(solution)/shard_map/all_gather | solution.py:85
  217.3 3.7 copy-start.3
  217.3 4.1 copy-start.4
  303.7 189.0 %all-to-all-start = ((f32[2,2048,512]{2,0,1:T(2,128)}), f32[2,2048,512]{2,0,1:T(2,128)}, u32[]{:S(2)}, u32[]{:S(2)}) async-start(f32[2,2048,512]{2,0,1:T(2,128)} %copy.148), calls=%async_computation | async-start | bytes 16777216 | tf_op jit(solution)/shard_map/all_to_all | solution.py:103
  519.5 9.7 copy-start.1
  540.8 3.1 copy-start.2
  545.6 9.1 copy-start
  582.1 188.8 %all-to-all-start.1 = ((f32[2,256,4096]{1,0,2:T(2,128)}), f32[2,256,4096]{1,0,2:T(2,128)}, u32[]{:S(2)}, u32[]{:S(2)}) async-start(f32[2,256,4096]{1,0,2:T(2,128)} %copy_dynamic-update-slice_fusion), calls=%async_computation.1 | async-start | bytes 16777216 | tf_op jit(solution)/shard_map/all_to_all | solution.py:123
  587.0 486.5 %reduce-scatter.2.cloned.1.call-start = ((), (), s32[]{:S(2)}) async-start(), calls=%async_computation.4 | async-start | bytes 20971520 | tf_op jit(solution)/shard_map/reduce_scatter | solution.py:131
Sparse Core Ops, SparseCore 0:
  9.2 160.0 all-gather.1
  922.0 151.5 reduce-scatter.1
where the time goes:
time: 1100 us; the launch traced here: 1090 us
  waiting for transfers between devices  630 us (57%)
  local copies, waits for them, and re-layouts  178 us (16%)
  matrix products  158 us (14%)
  other arithmetic  91.9 us (8%)
  between operations  19.3 us (2%)
    all_to_all x1, waiting for transfers between devices, on_device(): lax.all_to_all(padded, 'row', split_axis=2, concat_axis=1, tiled=True)  171 us
    all_to_all x1, waiting for transfers between devices, on_device(): lax.all_to_all(stacked, 'row', split_axis=1, concat_axis=2, tiled=True)  165 us
    reduce_scatter x1, waiting for transfers between devices, on_device(): summed = lax.psum_scatter(embedded, 'led', scatter_dimension=1, tiled=True)  152 us
    all_gather x1, waiting for transfers between devices, on_device(): region = lax.all_gather(spectrum, 'led', axis=1, tiled=True)  141 us
    dot_general x4, matrix products, transform(): jnp.einsum('p' + middle + ',pqkrj->q' + output, middle_pair, second_table...  79.1 us
    dot_general x4, matrix products, transform(): jnp.einsum('p' + inputs + ',pqtk->q' + middle, paired, first_table, preci...  78.8 us
    sub x1, other arithmetic, on_device(): lit_re = pupil_re * band_rows[0] - pupil_im * band_rows[1]  26.9 us
    another operation x4, local copies, waits for them, and re-layouts, on_device(): jnp.stack([lit_re, lit_im]).reshape(shape_rows)  24.9 us
  transfers between devices with their start and end apart: 4, of which 4 were waited for; matrix products, arithmetic and copies ran while one was open for 4% of the time, Pallas kernels for 0%

commit v1 on v0

--- a/solution.py
+++ b/solution.py
@@ -6,6 +6,31 @@
 
 SOFTENING = 0.1
 HIGHEST_PRECISION = lax.Precision.HIGHEST
+
+
+def treat_packet(z_in, array_axis):
+    mid_arr = list(z_in.shape[1:])
+    mid_arr[array_axis] *= z_in.shape[0]
+    outcome_arr = jnp.moveaxis(z_in, 0, array_axis).reshape(mid_arr)
+    return outcome_arr
+
+
+def derive_the_pairs_all(sheet, mesh_dim):
+    reply, part_next = (jax.lax.axis_size(mesh_dim), jax.lax.axis_index(mesh_dim))
+    r_now, block_last = (sheet[None], 1)
+    while block_last < reply:
+        m_next = jax.lax.ppermute(r_now, mesh_dim, perm=[(h, h ^ block_last) for h in range(reply)])
+        part_now = part_next & block_last == 0
+        r_now = jnp.concatenate(
+            [jnp.where(part_now, r_now, m_next), jnp.where(part_now, m_next, r_now)]
+        )
+        block_last *= 2
+    return r_now
+
+
+def obtain_page(shard_in, vector, array_dim):
+    w1 = treat_packet(derive_the_pairs_all(shard_in, vector), array_dim)
+    return w1
 
 
 def pupil_at(down_index, across_index, coeffs, centre):
@@ -82,7 +107,7 @@
     col_shift = offsets[led_index, 1]
     measured = amplitudes[0]
     shape_cols = (2, block_rows, outer_cols, row_count)
-    region = lax.all_gather(spectrum, "led", axis=1, tiled=True)
+    region = obtain_page(spectrum, "led", 1)
     band_rows = lax.dynamic_slice_in_dim(region, row_shift, window, 1)
     row_ids = jnp.arange(window, dtype=jnp.int32)[:, None]
     col_ids = (row_index * size_cols + jnp.arange(size_cols, dtype=jnp.int32))[None, :] - col_shift

time: 1100 us -> 1230 us (1.12)
  waiting for transfers between devices: 630 us -> 739 us
  other arithmetic: 91.9 us -> 116 us
    ppermute x0 -> x2, waiting for transfers between devices: none -> 250 us  [derive_the_pairs_all(): jax.lax.ppermute(r_now, mesh_dim, perm=[(h, h ^ block_last) for h in rang...]
    all_gather x1 -> x0, waiting for transfers between devices: 141 us -> none  [on_device(): region = lax.all_gather(spectrum, 'led', axis=1, tiled=True)]
    select_n x0 -> x2, other arithmetic: none -> 13.8 us  [derive_the_pairs_all(): jnp.where(part_now, r_now, m_next)]
  transfers between devices with their start and end apart: 4 -> 5, of which waited for: 4 -> 5; matrix products, arithmetic and copies ran while one was open for 4% -> 4% of each run, Pallas kernels for 0% -> 0%
where the time goes in v1:
time: 1230 us
  waiting for transfers between devices  739 us (60%)
  local copies, waits for them, and re-layouts  182 us (15%)
  matrix products  158 us (13%)
  other arithmetic  116 us (9%)
  between operations  19.1 us (2%)
  starting transfers between devices  14.9 us (1%)
    ppermute x2, waiting for transfers between devices, derive_the_pairs_all(): jax.lax.ppermute(r_now, mesh_dim, perm=[(h, h ^ block_last) for h in rang...  250 us
    all_to_all x1, waiting for transfers between devices, on_device(): lax.all_to_all(padded, 'row', split_axis=2, concat_axis=1, tiled=True)  171 us
    all_to_all x1, waiting for transfers between devices, on_device(): lax.all_to_all(stacked, 'row', split_axis=1, concat_axis=2, tiled=True)  165 us
    reduce_scatter x1, waiting for transfers between devices, on_device(): summed = lax.psum_scatter(embedded, 'led', scatter_dimension=1, tiled=True)  153 us
    dot_general x4, matrix products, transform(): jnp.einsum('p' + middle + ',pqkrj->q' + output, middle_pair, second_table...  79.1 us
    dot_general x4, matrix products, transform(): jnp.einsum('p' + inputs + ',pqtk->q' + middle, paired, first_table, preci...  78.8 us
    sub x1, other arithmetic, on_device(): lit_re = pupil_re * band_rows[0] - pupil_im * band_rows[1]  25.7 us
    another operation x4, local copies, waits for them, and re-layouts, on_device(): jnp.stack([lit_re, lit_im]).reshape(shape_rows)  24.6 us
  transfers between devices with their start and end apart: 5, of which 5 were waited for; matrix products, arithmetic and copies ran while one was open for 4% of the time, Pallas kernels for 0%

profile of v1, /device:TPU:0, one launch (start us, length us, event | category | flops | bytes accessed | tf_op | source)
XLA Modules:
  0.0 1228.4 jit_solution(14226821160376363154)
XLA Ops:
  6.5 3.0 collective-permute-start
  9.5 90.9 %collective-permute-done = f32[1,2,1024,512]{3,2,1,0:T(8,128)} collective-permute-done((f32[1,2,1024,512]{3,2,1,0:T(8,128)}, f32[1,2,1024,512]{3,2,1,0:T(8,128)}, u32[]{:S(2)}, u32[]{:S(2)}) %collective-permute-start) | collective-permute-done | bytes 4194336 | tf_op jit(solution)/shard_map/ppermute | solution.py:22
  100.4 4.5 broadcast_select_fusion.3
  104.9 4.7 pad_maximum_fusion
  109.6 1.0 copy-done.2
  110.7 1.8 collective-permute-start.1
  117.0 3.7 copy.152
  123.2 3.9 fusion.69
  127.1 4.1 multiply_sine_fusion
  131.3 2.0 maximum_bitcast_fusion.16
  133.2 159.4 %collective-permute-done.1 = f32[2,2,1024,512]{3,2,1,0:T(8,128)} collective-permute-done((f32[2,2,1024,512]{3,2,1,0:T(8,128)}, f32[2,2,1024,512]{3,2,1,0:T(8,128)}, u32[]{:S(2)}, u32[]{:S(2)}) %collective-permute-start.1) | collective-permute-done | bytes 8388640 | tf_op jit(solution)/shard_map/ppermute | solution.py:22
  292.6 9.3 broadcast_select_fusion.1
  301.9 7.0 maximum_bitcast_fusion
  309.0 1.9 copy.149
  310.9 25.7 %multiply_subtract_fusion = (f32[1,2048,512]{2,1,0:T(8,128)}, f32[1,2048,512]{2,1,0:T(8,128)}) fusion(f32[2,4096,512]{2,1,0:T(8,128)S(1)} %bitcast.192, s32[]{:T(128)S(6)} %select_n.268, s32[]{:T(128)S(6)} %add.718, f32[]{:T(128)} %bitcast.6, f32[512]{0:T(512)S(1)} %get-tuple-element.57, f32[2048]{0:T(1024)S(1)} %get-tuple-element.62, ...), kind=kLoop, calls=%fused_computation.57 | loop fusion | flops 33554432 | bytes 16818200 | tf_op jit(solution)/shard_map/sub | solution.py:115
  336.6 7.7 stack.215
  344.3 5.6 copy.150
  349.8 7.7 stack.216
  357.5 3.7 copy.151
  361.6 28.3 %fusion.46 = f32[2,512,4,512,1]{3,1,2,0,4:T(8,128)} fusion(f32[1,512,4,512]{3,1,0,2:T(8,128)S(1)} %copy.151, f32[1,512,4,512]{3,1,0,2:T(8,128)S(1)} %copy-done.7, f32[1,2,512,512]{2,3,0,1:T(8,128)S(1)} %copy-done.8, f32[1,2,512,512]{2,3,0,1:T(8,128)S(1)} %get-tuple-element.21), kind=kOutput, calls=%fused_computation.62 | convolution fusion | flops 25772949504 | bytes 20971520 | tf_op jit(solution)/shard_map/ptrc,pqtk->qkrc/dot_general | solution.py:80
  390.0 32.7 %fusion.11 = f32[2,4,512,512]{3,1,0,2:T(4,128)S(1)} fusion(f32[2,2,512,4,4]{3,4,0,1,2:T(4,128)} %copy.152, f32[2,512,4,512,1]{3,1,2,0,4:T(8,128)} %fusion.46), kind=kOutput, calls=%fused_computation.21 | convolution fusion | flops 201326592 | bytes 16908288 | tf_op jit(solution)/shard_map/pkrc,pqkrj->qjkc/dot_general | solution.py:83
  422.6 4.9 copy.154
  427.5 16.5 %copy.155 = f32[2,2048,512]{2,0,1:T(2,128)} copy(f32[2,2048,512]{2,1,0:T(8,128)S(1)} %bitcast.193) | data formatting | bytes 16777216 | tf_op jit(solution)/shard_map/reshape | solution.py:127
  444.0 5.1 all-to-all-start
  450.9 4.4 copy.159
  455.3 1.9 copy.163
  457.2 4.4 copy.167
  464.2 1.0 multiply_sine_fusion.2
  465.3 1.0 multiply_sine_fusion.3
  466.3 1.1 maximum_bitcast_fusion.23
  467.5 165.5 %all-to-all-done = f32[2,2048,512]{2,0,1:T(2,128)} async-done(((f32[2,2048,512]{2,0,1:T(2,128)}), f32[2,2048,512]{2,0,1:T(2,128)}, u32[]{:S(2)}, u32[]{:S(2)}) %all-to-all-start) | async-done | bytes 8388640 | tf_op jit(solution)/shard_map/all_to_all | solution.py:128
  633.0 8.2 copy.156
  641.2 8.8 copy.157
  650.0 4.5 dynamic-slice_bitcast_fusion
  654.5 5.3 copy.158
  659.8 9.7 fusion.54
  669.6 7.0 fusion.47
  678.3 2.7 fusion.57
  681.0 3.1 copy.164
  684.1 1.8 copy.165
  685.9 9.1 fusion.53
  695.0 7.0 fusion.50
  702.0 2.4 copy.169
  704.5 5.5 broadcast_in_dim.17
  709.9 12.4 %copy_dynamic-update-slice_fusion = f32[2,256,4096]{1,0,2:T(2,128)} fusion(f32[2,256,4096]{1,0,2:T(2,128)} %broadcast_in_dim.17, s32[]{:T(128)S(6)} %select_n.269, f32[2,256,2048]{1,2,0:T(8,128)S(1)} %bitcast.198), kind=kLoop, calls=%fused_computation.54 | loop fusion | bytes 8388612 | tf_op jit(solution)/shard_map/dynamic_update_slice | solution.py:145
  722.4 4.9 all-to-all-start.1
  727.4 3.3 copy.175
  730.7 3.9 fusion.68
  734.6 4.1 multiply_sine_fusion.1
  738.7 1.9 maximum_bitcast_fusion.14
  740.7 170.5 %all-to-all-done.1 = f32[2,256,4096]{1,0,2:T(2,128)} async-done(((f32[2,256,4096]{1,0,2:T(2,128)}), f32[2,256,4096]{1,0,2:T(2,128)}, u32[]{:S(2)}, u32[]{:S(2)}) %all-to-all-start.1) | async-done | bytes 8388640 | tf_op jit(solution)/shard_map/all_to_all | solution.py:148
  911.2 7.3 copy.171
  918.5 13.3 %copy.172 = f32[2,8,256,512]{3,0,2,1:T(2,128)} copy(f32[2,8,256,512]{2,3,1,0:T(8,128)} %bitcast.195) | data formatting | bytes 16777216 | tf_op jit(solution)/shard_map/all_to_all | solution.py:148
  931.8 31.6 %fusion.41 = f32[2,512,4,512,1]{3,1,2,0,4:T(8,128)} fusion(f32[2,512,4,512]{3,0,2,1:T(2,128)} %bitcast.199, f32[1,2,512,512]{2,3,1,0:T(8,128)} %get-tuple-element.20, f32[1,2,512,512]{2,3,1,0:T(8,128)S(1)} %get-tuple-element.19), kind=kOutput, calls=%fused_computation.61 | convolution fusion | flops 25770852352 | bytes 20971520 | tf_op jit(solution)/shard_map/ptrc,pqtk->qkrc/dot_general | solution.py:80
  963.4 32.4 %fusion.14 = f32[2,4,512,512]{3,1,0,2:T(4,128)S(1)} fusion(f32[2,2,512,4,4]{3,4,0,1,2:T(4,128)} %copy.175, f32[2,512,4,512,1]{3,1,2,0,4:T(8,128)} %fusion.41), kind=kOutput, calls=%fused_computation.22 | convolution fusion | flops 201326592 | bytes 16908288 | tf_op jit(solution)/shard_map/pkrc,pqkrj->qjkc/dot_general | solution.py:83
  995.9 3.5 fusion.91
  999.3 3.5 copy.177
  1002.9 1.4 copy.178
  1004.2 23.0 %fusion.32 = (f32[1,2048,512]{2,1,0:T(8,128)S(1)}, f32[1,2048,512]{2,1,0:T(8,128)S(1)}) fusion(f32[1,4,512,512]{3,2,1,0:T(8,128)S(1)} %copy.178, f32[1,4,512,512]{3,2,1,0:T(8,128)S(1)} %copy.177, f32[]{:T(128)} %bitcast.6, f32[512]{0:T(512)S(1)} %get-tuple-element.57, f32[2048]{0:T(1024)S(1)} %get-tuple-element.62, f32[512]{0:T(512)S(1)} %get-tuple-element.58, ...), kind=kLoop, calls=%fused_computation.43 | loop fusion | flops 33554432 | bytes 16818192 | tf_op jit(solution)/shard_map/add | solution.py:152
  1027.3 4.3 pad_maximum_fusion.1
  1031.5 7.9 broadcast_in_dim.14
  1039.4 22.7 %dynamic_update_slice.7 = f32[2,4096,512]{2,1,0:T(8,128)} dynamic-update-slice(f32[2,4096,512]{2,1,0:T(8,128)} %broadcast_in_dim.14, f32[2,2048,512]{2,1,0:T(8,128)} %pad_maximum_fusion.1, s32[]{:T(128)} %constant.59.clone.1, s32[]{:T(128)S(6)} %select_n.268, s32[]{:T(128)} %constant.59.clone.1) | dynamic-update-slice | bytes 16777220 | tf_op jit(solution)/shard_map/dynamic_update_slice | solution.py:155
  1062.1 152.7 %reduce-scatter.2.cloned.1.call-done = f32[2,1024,512]{2,1,0:T(8,128)} async-done(((f32[2,4096,512]{2,1,0:T(8,128)}), f32[2,1024,512]{2,1,0:T(8,128)}) %reduce-scatter.2.cloned.1.call-update) | async-done | bytes 4194320 | tf_op jit(solution)/shard_map/reduce_scatter | solution.py:156
  1214.8 6.5 add.717
  (49 shorter events, 8.6 us)
Async XLA Ops:
  6.5 93.9 %collective-permute-start = (f32[1,2,1024,512]{3,2,1,0:T(8,128)}, f32[1,2,1024,512]{3,2,1,0:T(8,128)}, u32[]{:S(2)}, u32[]{:S(2)}) collective-permute-start(f32[1,2,1024,512]{3,2,1,0:T(8,128)} %bitcast.197), channel_id=1, source_target_pairs={{0,8},{8,0},{16,24},{24,16},{1,9},{9,1},{17,25},{25,17},{2,10},{10... | collective-permute-start | bytes 12582920 | tf_op jit(solution)/shard_map/ppermute | solution.py:22
  104.9 4.8 copy-start
  104.9 5.8 copy-start.2
  104.9 7.5 copy-start.10
  104.9 9.5 copy-start.9
  110.7 181.9 %collective-permute-start.1 = (f32[2,2,1024,512]{3,2,1,0:T(8,128)}, f32[2,2,1024,512]{3,2,1,0:T(8,128)}, u32[]{:S(2)}, u32[]{:S(2)}) collective-permute-start(f32[2,2,1024,512]{3,2,1,0:T(8,128)} %pad_maximum_fusion), channel_id=1, source_target_pairs={{0,16},{8,24},{16,0},{24,8},{1,17},{9,25},{17,1},{25,9},{2,18},{10... | collective-permute-start | bytes 25165832 | tf_op jit(solution)/shard_map/ppermute | solution.py:22
  127.1 165.5 %copy-start.3 = (f32[1,2,1024,512]{3,2,1,0:T(8,128)S(1)}, f32[1,2,1024,512]{3,2,1,0:T(8,128)}, u32[]{:S(2)}) copy-start(f32[1,2,1024,512]{3,2,1,0:T(8,128)} %copy-done.2) | copy-start | bytes 12582916
  131.3 161.4 %copy-start.1 = (f32[1,2,1024,512]{3,2,1,0:T(8,128)S(1)}, f32[1,2,1024,512]{3,2,1,0:T(8,128)}, u32[]{:S(2)}) copy-start(f32[1,2,1024,512]{3,2,1,0:T(8,128)} %copy-done) | copy-start | bytes 12582916
  357.5 3.7 copy-start.7
  357.5 4.1 copy-start.8
  444.0 189.0 %all-to-all-start = ((f32[2,2048,512]{2,0,1:T(2,128)}), f32[2,2048,512]{2,0,1:T(2,128)}, u32[]{:S(2)}, u32[]{:S(2)}) async-start(f32[2,2048,512]{2,0,1:T(2,128)} %copy.155), calls=%async_computation | async-start | bytes 16777216 | tf_op jit(solution)/shard_map/all_to_all | solution.py:128
  659.8 9.7 copy-start.5
  681.0 3.1 copy-start.6
  685.9 9.1 copy-start.4
  722.4 188.8 %all-to-all-start.1 = ((f32[2,256,4096]{1,0,2:T(2,128)}), f32[2,256,4096]{1,0,2:T(2,128)}, u32[]{:S(2)}, u32[]{:S(2)}) async-start(f32[2,256,4096]{1,0,2:T(2,128)} %copy_dynamic-update-slice_fusion), calls=%async_computation.1 | async-start | bytes 16777216 | tf_op jit(solution)/shard_map/all_to_all | solution.py:148
  727.3 487.5 %reduce-scatter.2.cloned.1.call-start = ((), (), s32[]{:S(2)}) async-start(), calls=%async_computation.3 | async-start | bytes 20971520 | tf_op jit(solution)/shard_map/reduce_scatter | solution.py:156
Sparse Core Ops, SparseCore 0:
  1062.2 152.5 reduce-scatter.1
